TPU v7x, 512 devices: a whole 4x8x8 slice. The times are simulated.
512 devices in a mesh: req: 128 (over z, y, core), grp: 4 (over x).
Axes of the slice: x: 4, y: 8, z: 8, core: 2. Of those that a mesh axis runs over, the one named last changes fastest.
Arguments:
- owner_slab: bfloat16 [65536, 1024], P('req'), may hold values from -6 to 6
- segment_ids: int32 [128, 512], P('req'), may hold values from 0 to 511, as said below
- head_weights: bfloat16 [1024, 16, 192], P(None, 'grp')
- merge_weights: bfloat16 [16, 64, 1024], P('grp'), may hold values from -0.1875 to 0.1875
- first_gain: float32 [1024], replicated, may hold values from 0.25 to 1.75
- first_bias: float32 [1024], replicated, may hold values from -3 to 3
- up_weights: bfloat16 [1024, 4096], P('req', 'grp'), may hold values from -0.1875 to 0.1875
- down_weights: bfloat16 [4096, 1024], P('grp', 'req'), may hold values from -0.09375 to 0.09375
- second_gain: float32 [1024], replicated, may hold values from 0.25 to 1.75
- second_bias: float32 [1024], replicated, may hold values from -3 to 3
- page_table: int32 [128, 4], P('req'), may hold values from 0 to 3, each once within a row
- row_map: int32 [128, 4, 128], P('req', 'grp'), may hold values from 0 to 127, each once within a row
Outputs:
- layer_out: bfloat16 [65536, 1024], P(('req', 'grp'))
- cache_pages: bfloat16 [512, 128, 16, 128], P('req', None, 'grp')
Inputs may be any that keep to these rules, and one draw needn't show every extreme that they name: `segment_ids`: within each slab the ids start at 0, never fall and rise by at most one from row to row; in one slab all 512 rows form a single request, and in one other slab every row is a request of its own.
All inputs are finite; a program needn't handle non-finite values.
Results may differ from a plain program's by a relative error of at most 0.0075.
Values may be sent and summed in bfloat16 or wider, within the bound.
No kernel may reach another device: no remote copies, remote signals or barrier semaphores. Data moves between devices by JAX's collectives and lax.ppermute only.
A program may use at most 64 MiB of HBM per device.

v0:
```python
import math
import jax
import jax.numpy as jnp
from jax import lax
from jax.sharding import PartitionSpec as P

EPSILON = 1e-05


def layer_norm(values, gain, bias):
    center = values - jnp.mean(values, axis=-1, keepdims=True)
    spread = jnp.mean(center * center, axis=-1, keepdims=True)
    return center * lax.rsqrt(spread + EPSILON) * gain + bias


def local(
    owner_slab,
    segment_ids,
    head_weights,
    merge_weights,
    first_gain,
    first_bias,
    up_weights,
    down_weights,
    second_gain,
    second_bias,
    page_table,
    row_map,
):
    group = lax.axis_size("grp")
    owners = lax.axis_size("req")
    rows_all = owner_slab.shape[0]
    width = owner_slab.shape[1]
    quarter = rows_all // group
    local_heads = head_weights.shape[1]
    head_dim = head_weights.shape[2] // 3
    projected = jnp.einsum(
        "nd,dhc->nhc", owner_slab, head_weights, preferred_element_type=jnp.float32
    ).astype(jnp.bfloat16)
    queries = jnp.moveaxis(projected[:, :, :head_dim], 1, 0)
    key_rows = jnp.moveaxis(projected[:, :, head_dim : 2 * head_dim], 1, 0)
    value_rows = jnp.moveaxis(projected[:, :, 2 * head_dim :], 1, 0)
    segment = segment_ids[0]
    position = jnp.arange(rows_all, dtype=jnp.int32)
    allowed = (position[:, None] >= position[None, :]) & (segment[:, None] == segment[None, :])
    scale = 1.0 / math.sqrt(head_dim)

    def one_head(operands):
        query_head, key_head, value_head = operands
        scores = (
            lax.dot_general(
                query_head, key_head, (((1,), (1,)), ((), ())), preferred_element_type=jnp.float32
            )
            * scale
        )
        scores = jnp.where(allowed, scores, -1e30)
        probs = jax.nn.softmax(scores, axis=-1).astype(jnp.bfloat16)
        return jnp.dot(probs, value_head, preferred_element_type=jnp.float32).astype(jnp.bfloat16)

    attended = jnp.moveaxis(lax.map(one_head, (queries, key_rows, value_rows)), 0, 1)
    own = lax.axis_index("grp")
    own_rows = lax.dynamic_slice_in_dim(owner_slab, own * quarter, quarter, 0).astype(jnp.float32)
    partial_rows = jnp.einsum(
        "nhd,hde->ne", attended, merge_weights, preferred_element_type=jnp.float32
    )
    mixed = lax.psum_scatter(partial_rows, "grp", scatter_dimension=0, tiled=True)
    hidden = layer_norm(own_rows + mixed, first_gain, first_bias).astype(jnp.bfloat16)
    slots = quarter // owners
    placed = jnp.zeros_like(hidden).at[row_map[0, 0]].set(hidden)
    arrived = lax.all_to_all(
        placed.reshape(owners, slots, width), "req", split_axis=0, concat_axis=0, tiled=True
    )
    even_rows = arrived.reshape(quarter, width)
    group_rows = lax.all_gather(even_rows, "grp", axis=0, tiled=True)
    raised = jnp.dot(
        group_rows,
        lax.all_gather(up_weights, "req", axis=0, tiled=True),
        preferred_element_type=jnp.float32,
    )
    activated = jax.nn.gelu(raised, approximate=False).astype(jnp.bfloat16)
    lowered_all = jnp.dot(
        activated,
        lax.all_gather(down_weights, "req", axis=1, tiled=True),
        preferred_element_type=jnp.float32,
    )
    lowered = lax.psum_scatter(lowered_all, "grp", scatter_dimension=0, tiled=True)
    layer_out = layer_norm(
        even_rows.astype(jnp.float32) + lowered, second_gain, second_bias
    ).astype(jnp.bfloat16)
    page_count = page_table.shape[1]
    page_rows = rows_all // page_count
    stacked = projected[:, :, head_dim:].reshape(page_count, page_rows, local_heads, 2 * head_dim)
    cache_pages = jnp.zeros_like(stacked).at[page_table[0]].set(stacked)
    return (layer_out, cache_pages)


def solution(mesh):
    in_specs = (
        P("req", None),
        P("req", None),
        P(None, "grp", None),
        P("grp", None, None),
        P(),
        P(),
        P("req", "grp"),
        P("grp", "req"),
        P(),
        P(),
        P("req", None),
        P("req", "grp", None),
    )
    out_specs = (P(("req", "grp"), None), P("req", None, "grp", None))
    return jax.shard_map(local, mesh=mesh, in_specs=in_specs, out_specs=out_specs, check_vma=False)
```

profile of v0, /device:TPU:1, one launch (start us, length us, event | category | flops | bytes accessed | tf_op | source)
XLA Modules:
  0.0 281.3 jit_solution(15280526608803334837)
XLA Ops:
  8.1 1.3 copy-done
  9.4 2.2 fusion.105
  12.3 3.7 %while.11 = (s32[]{:T(128)}, bf16[4,512,64]{1,2,0:T(8,128)(2,1)S(1)}, bf16[4,512,64]{1,2,0:T(8,128)(2,1)S(1)}, bf16[4,512,64]{1,2,0:T(8,128)(2,1)S(1)}, bf16[4,5...) while((s32[]{:T(128)}, bf16[4,512,64]{1,2,0:T(8,128)(2,1)S(1)}, ...), condition=%wide.region_3.4_spmd.clone, body=%wide.region_0.3_spmd.clone.sunk | while | flops 70024192 | bytes 3424341 | solution.py:60
  16.1 0.7 copy-done.10
  16.8 3.0 %convolution_bitcast_fusion = f32[512,1024]{1,0:T(8,128)} fusion(bf16[4,64,1024]{2,1,0:T(8,128)(2,1)} %param.17, bf16[4,512,64]{1,2,0:T(8,128)(2,1)} %copy-done.10), kind=kOutput, calls=%fused_computation.40 | convolution fusion | flops 268435456 | bytes 2883584 | tf_op jit(solution)/shard_map/nhd,hde->ne/dot_general | solution.py:63
  19.9 0.5 all-gather.5.cloned.1.call-update
  20.4 0.5 all-gather.7.cloned.1.call-update
  21.1 39.4 %reduce-scatter.3.cloned.1.call-done = f32[128,1024]{1,0:T(8,128)} async-done(((f32[512,1024]{1,0:T(8,128)}), f32[128,1024]{1,0:T(8,128)}) %reduce-scatter.3.cloned.1.call-update) | async-done | bytes 524304 | tf_op jit(solution)/shard_map/reduce_scatter | solution.py:66
  60.4 1.2 fusion.70
  61.6 1.2 multiply_reduce_fusion.1
  62.9 1.9 scatter_custom_fusion
  65.3 0.8 reduce
  66.3 30.1 %all_to_all.5 = bf16[128,2,512]{2,1,0:T(2,128)(2,1)S(1)} all-to-all(bf16[128,2,512]{2,1,0:T(2,128)(2,1)S(1)} %reshape.126), channel_id=1, replica_groups=mesh['req'=128,'grp'=4] {'req'}, dimensions={0} | all-to-all | bytes 524288 | tf_op jit(solution)/shard_map/all_to_all | solution.py:70
  96.6 0.8 copy.29
  97.7 16.5 %all-gather.5.cloned.1.call-done = bf16[1024,1024]{1,0:T(8,128)(2,1)} async-done(((bf16[8,1024]{1,0:T(8,128)(2,1)}), bf16[1024,1024]{1,0:T(8,128)(2,1)}) %all-gather.5.cloned.1.call-update) | async-done | bytes 2097168 | tf_op jit(solution)/shard_map/all_gather | solution.py:77
  114.2 82.0 %all-gather.7.cloned.1.call-done = bf16[1024,1024]{0,1:T(8,128)(2,1)} async-done(((bf16[1024,8]{0,1:T(8,128)(2,1)}), bf16[1024,1024]{0,1:T(8,128)(2,1)}) %all-gather.7.cloned.1.call-update) | async-done | bytes 2097168 | tf_op jit(solution)/shard_map/all_gather | solution.py:83
  196.1 26.4 %all-gather.9.cloned.1.call-done = bf16[512,1,1024]{2,0,1:T(8,128)(2,1)} async-done(((bf16[128,1,1024]{2,0,1:T(8,128)(2,1)}), bf16[512,1,1024]{2,0,1:T(8,128)(2,1)}) %all-gather.9.cloned.1.call-update) | async-done | bytes 1048592 | tf_op jit(solution)/shard_map/all_gather | solution.py:74
  222.5 10.1 %fusion.25 = f32[512,1024]{1,0:T(8,128)} fusion(bf16[1024,1024]{0,1:T(8,128)(2,1)} %all-gather.7.cloned.1.call-done, bf16[1024,1024]{1,0:T(8,128)(2,1)} %all-gather.5.cloned.1.call-done, bf16[512,1,1024]{2,0,1:T(8,128)(2,1)} %all-gather.9.cloned.1.call-done), kind=kOutput, calls=%fused_computation.41 | convolution fusion | flops 2181562368 | bytes 7340032 | tf_op jit(solution)/shard_map/dot_general | solution.py:81
  233.4 0.8 scatter_fusion
  234.2 1.2 copy.32
  235.4 34.8 %reduce-scatter.5.cloned.1.call-done = f32[128,1024]{1,0:T(8,128)} async-done(((f32[512,1024]{1,0:T(8,128)}), f32[128,1024]{1,0:T(8,128)}) %reduce-scatter.5.cloned.1.call-update) | async-done | bytes 524304 | tf_op jit(solution)/shard_map/reduce_scatter | solution.py:86
  270.2 1.3 fusion.69
  271.5 1.3 multiply_reduce_fusion
  272.8 0.9 add_convert_fusion
  (56 shorter events, 6.5 us)
Async XLA Ops:
  8.0 1.4 copy-start
  8.0 52.4 %reduce-scatter.3.cloned.1.call-start = ((), (), s32[]{:S(2)}) async-start(), calls=%async_computation.3 | async-start | bytes 2621440 | tf_op jit(solution)/shard_map/reduce_scatter | solution.py:66
  11.6 0.7 copy-start.7
  16.1 0.7 copy-start.10
  16.8 4.3 %copy-start.8 = (s32[1,1,128]{2,1,0:T(1,128)S(1)}, s32[1,1,128]{2,1,0:T(1,128)}, u32[]{:S(2)}) copy-start(s32[1,1,128]{2,1,0:T(1,128)} %param.25) | copy-start | bytes 1540
  16.8 43.6 %copy-start.2 = (bf16[512,1024]{1,0:T(8,128)(2,1)S(1)}, bf16[512,1024]{1,0:T(8,128)(2,1)}, u32[]{:S(2)}) copy-start(bf16[512,1024]{1,0:T(8,128)(2,1)} %param.14) | copy-start | bytes 3145732
  19.8 43.1 %copy-start.3 = (f32[1024]{0:T(1024)S(1)}, f32[1024]{0:T(1024)}, u32[]{:S(2)}) copy-start(f32[1024]{0:T(1024)} %param.19) | copy-start | bytes 12292
  19.8 43.1 %copy-start.4 = (f32[1024]{0:T(1024)S(1)}, f32[1024]{0:T(1024)}, u32[]{:S(2)}) copy-start(f32[1024]{0:T(1024)} %param.18) | copy-start | bytes 12292
  19.8 94.3 %all-gather.5.cloned.1.call-start = ((), (), s32[]{:S(2)}) async-start(), calls=%async_computation.4 | async-start | bytes 2113536 | tf_op jit(solution)/shard_map/all_gather | solution.py:77
  20.4 175.7 %all-gather.7.cloned.1.call-start = ((), (), s32[]{:S(2)}) async-start(), calls=%async_computation.5 | async-start | bytes 2113536 | tf_op jit(solution)/shard_map/all_gather | solution.py:83
  21.0 201.5 %all-gather.9.cloned.1.call-start = ((), (), s32[]{:S(2)}) async-start(), calls=%async_computation.7 | async-start | bytes 1310720 | tf_op jit(solution)/shard_map/all_gather | solution.py:74
  97.4 172.8 %reduce-scatter.5.cloned.1.call-start = ((), (), s32[]{:S(2)}) async-start(), calls=%async_computation.6 | async-start | bytes 2621440 | tf_op jit(solution)/shard_map/reduce_scatter | solution.py:86
  232.6 0.7 copy-start.9
  233.4 39.4 %copy-start.5 = (f32[1024]{0:T(1024)S(1)}, f32[1024]{0:T(1024)}, u32[]{:S(2)}) copy-start(f32[1024]{0:T(1024)} %param.23) | copy-start | bytes 12292
  233.4 39.4 %copy-start.6 = (f32[1024]{0:T(1024)S(1)}, f32[1024]{0:T(1024)}, u32[]{:S(2)}) copy-start(f32[1024]{0:T(1024)} %param.22) | copy-start | bytes 12292
  270.2 2.6 copy-start.1
Sparse Core Ops, SparseCore 0:
  19.9 40.4 reduce-scatter.2
  232.8 37.4 reduce-scatter.4
Sparse Core Ops, SparseCore 1:
  23.4 90.7 all-gather.4
  117.2 78.9 all-gather.6
  198.7 23.8 all-gather.8
where the time goes:
time: 282 us; the launch traced here: 281 us
  waiting for transfers between devices  200 us (71%)
  blocking collectives  30.1 us (11%)
  matrix products  18.2 us (6%)
  between operations  15.9 us (6%)
  other arithmetic  9.46 us (3%)
  local copies, waits for them, and re-layouts  7.03 us (2%)
    all_gather x1, waiting for transfers between devices, local(): lax.all_gather(down_weights, 'req', axis=1, tiled=True)  82 us
    reduce_scatter x1, waiting for transfers between devices, local(): lax.psum_scatter(partial_rows, 'grp', scatter_dimension=0, tiled=True)  39.4 us
    reduce_scatter x1, waiting for transfers between devices, local(): lax.psum_scatter(lowered_all, 'grp', scatter_dimension=0, tiled=True)  34.8 us
    all_to_all x1, blocking collectives, local(): lax.all_to_all(placed.reshape(owners, slots, width), 'req', split_axis=0,...  30.1 us
    all_gather x1, waiting for transfers between devices, local(): group_rows = lax.all_gather(even_rows, 'grp', axis=0, tiled=True)  26.4 us
    all_gather x1, waiting for transfers between devices, local(): lax.all_gather(up_weights, 'req', axis=0, tiled=True)  16.5 us
    dot_general x1, matrix products, local(): jnp.dot(activated, lax.all_gather(down_weights, 'req', axis=1, tiled=True...  10.1 us
  transfers between devices with their start and end apart: 5, of which 5 were waited for; matrix products, arithmetic and copies ran while one was open for 3% of the time, Pallas kernels for 0%

commit v1 on v0

--- a/solution.py
+++ b/solution.py
@@ -5,6 +5,19 @@
 from jax.sharding import PartitionSpec as P
 
 EPSILON = 1e-05
+
+
+def ring_gather(x, axis, dim):
+    ways = lax.axis_size(axis)
+    up = [(d, (d + 1) % ways) for d in range(ways)]
+    down = [(d, (d - 1) % ways) for d in range(ways)]
+    earlier, later = ([x], [x])
+    for _ in range(ways // 2):
+        earlier.append(lax.ppermute(earlier[-1], axis, up))
+    for _ in range((ways - 1) // 2):
+        later.append(lax.ppermute(later[-1], axis, down))
+    line = jnp.concatenate([*earlier[::-1], *later[1:]], axis=dim)
+    return jnp.roll(line, (lax.axis_index(axis) - ways // 2) * x.shape[dim], axis=dim)
 
 
 def layer_norm(values, gain, bias):
@@ -71,7 +84,7 @@
         placed.reshape(owners, slots, width), "req", split_axis=0, concat_axis=0, tiled=True
     )
     even_rows = arrived.reshape(quarter, width)
-    group_rows = lax.all_gather(even_rows, "grp", axis=0, tiled=True)
+    group_rows = ring_gather(even_rows, "grp", 0)
     raised = jnp.dot(
         group_rows,
         lax.all_gather(up_weights, "req", axis=0, tiled=True),

time: 282 us -> 249 us (0.88)
  waiting for transfers between devices: 200 us -> 153 us
  starting transfers between devices: 0.38 us -> 8.73 us
  local copies, waits for them, and re-layouts: 7.03 us -> 13 us
    all_gather x1 -> x0, waiting for transfers between devices: 26.4 us -> none  [local(): group_rows = lax.all_gather(even_rows, 'grp', axis=0, tiled=True)]
    all_gather x1, waiting for transfers between devices: 16.5 us -> 0.01 us  [local(): lax.all_gather(up_weights, 'req', axis=0, tiled=True)]
    ppermute x0 -> x3, waiting for transfers between devices: none -> 11.9 us  [the longest x2 11.9 us: ring_gather(): earlier.append(lax.ppermute(earlier[-1], axis, up))]
    all_gather x1, waiting for transfers between devices: 82 us -> 72.3 us  [local(): lax.all_gather(down_weights, 'req', axis=1, tiled=True)]
    ppermute x0 -> x3, starting transfers between devices: none -> 8.57 us  [the longest x1 4.75 us: ring_gather(): later.append(lax.ppermute(later[-1], axis, down))]
    unnamed x25 -> x33, local copies, waits for them, and re-layouts: 4.26 us -> 10.2 us
    reduce_scatter x1, waiting for transfers between devices: 34.8 us -> 28.9 us  [local(): lax.psum_scatter(lowered_all, 'grp', scatter_dimension=0, tiled=True)]
  transfers between devices with their start and end apart: 5 -> 7, of which waited for: 5 -> 5; matrix products, arithmetic and copies ran while one was open for 3% -> 6% of each run, Pallas kernels for 0% -> 0%
where the time goes in v1:
time: 249 us
  waiting for transfers between devices  153 us (61%)
  blocking collectives  30.1 us (12%)
  matrix products  18.2 us (7%)
  between operations  15.8 us (6%)
  local copies, waits for them, and re-layouts  13 us (5%)
  other arithmetic  9.46 us (4%)
  starting transfers between devices  8.73 us (4%)
    all_gather x1, waiting for transfers between devices, local(): lax.all_gather(down_weights, 'req', axis=1, tiled=True)  72.3 us
    reduce_scatter x1, waiting for transfers between devices, local(): lax.psum_scatter(partial_rows, 'grp', scatter_dimension=0, tiled=True)  39.3 us
    all_to_all x1, blocking collectives, local(): lax.all_to_all(placed.reshape(owners, slots, width), 'req', split_axis=0,...  30.1 us
    reduce_scatter x1, waiting for transfers between devices, local(): lax.psum_scatter(lowered_all, 'grp', scatter_dimension=0, tiled=True)  28.9 us
    ppermute x2, waiting for transfers between devices, ring_gather(): earlier.append(lax.ppermute(earlier[-1], axis, up))  11.9 us
    unnamed x33, local copies, waits for them, and re-layouts  10.2 us
    dot_general x1, matrix products, local(): jnp.dot(activated, lax.all_gather(down_weights, 'req', axis=1, tiled=True...  10.1 us
  transfers between devices with their start and end apart: 7, of which 5 were waited for; matrix products, arithmetic and copies ran while one was open for 6% of the time, Pallas kernels for 0%

profile of v1, /device:TPU:1, one launch (start us, length us, event | category | flops | bytes accessed | tf_op | source)
XLA Modules:
  0.0 248.8 jit_solution(7250108298290878919)
XLA Ops:
  8.1 1.3 copy-done
  9.4 2.2 fusion.107
  12.3 3.7 %while.11 = (s32[]{:T(128)}, bf16[4,512,64]{1,2,0:T(8,128)(2,1)S(1)}, bf16[4,512,64]{1,2,0:T(8,128)(2,1)S(1)}, bf16[4,512,64]{1,2,0:T(8,128)(2,1)S(1)}, bf16[4,5...) while((s32[]{:T(128)}, bf16[4,512,64]{1,2,0:T(8,128)(2,1)S(1)}, ...), condition=%wide.region_3.4_spmd.clone, body=%wide.region_0.3_spmd.clone.sunk | while | flops 70024192 | bytes 3424333 | solution.py:73
  16.8 3.0 %convolution_bitcast_fusion = f32[512,1024]{1,0:T(8,128)} fusion(bf16[4,64,1024]{2,1,0:T(8,128)(2,1)} %param.17, bf16[4,512,64]{1,2,0:T(8,128)(2,1)} %copy-done.10), kind=kOutput, calls=%fused_computation.40 | convolution fusion | flops 268435456 | bytes 2883584 | tf_op jit(solution)/shard_map/nhd,hde->ne/dot_general | solution.py:76
  21.1 39.3 %reduce-scatter.3.cloned.1.call-done = f32[128,1024]{1,0:T(8,128)} async-done(((f32[512,1024]{1,0:T(8,128)}), f32[128,1024]{1,0:T(8,128)}) %reduce-scatter.3.cloned.1.call-update) | async-done | bytes 524304 | tf_op jit(solution)/shard_map/reduce_scatter | solution.py:79
  60.4 1.2 fusion.70
  61.6 1.2 multiply_reduce_fusion.1
  62.9 1.9 scatter_custom_fusion
  65.3 0.8 reduce
  66.3 30.1 %all_to_all.5 = bf16[128,2,512]{2,1,0:T(2,128)(2,1)S(1)} all-to-all(bf16[128,2,512]{2,1,0:T(2,128)(2,1)S(1)} %reshape.124), channel_id=1, replica_groups=mesh['req'=128,'grp'=4] {'req'}, dimensions={0} | all-to-all | bytes 524288 | tf_op jit(solution)/shard_map/all_to_all | solution.py:83
  96.6 0.8 copy.45
  97.4 1.9 collective-permute-start
  99.3 8.9 %collective-permute-done = bf16[128,1024]{1,0:T(8,128)(2,1)S(1)} collective-permute-done((bf16[128,1024]{1,0:T(8,128)(2,1)}, bf16[128,1024]{1,0:T(8,128)(2,1)S(1)}, u32[]{:S(2)}, u32[]{:S(2)}) %collective-permute-start) | collective-permute-done | bytes 262176 | tf_op jit(solution)/shard_map/ppermute | solution.py:16
  108.2 1.9 collective-permute-start.1
  110.1 4.8 %collective-permute-start.2 = (bf16[128,1024]{1,0:T(8,128)(2,1)}, bf16[128,1024]{1,0:T(8,128)(2,1)S(1)}, u32[]{:S(2)}, u32[]{:S(2)}) collective-permute-start(bf16[128,1024]{1,0:T(8,128)(2,1)} %bitcast.62), channel_id=1, source_target_pairs={{0,3},{1,0},{2,1},{3,2},{4,7},{5,4},{6,5},{7,6},{8,11},{9,8},{10,9... | collective-permute-start | bytes 786440 | tf_op jit(solution)/shard_map/ppermute | solution.py:18
  114.9 3.0 %collective-permute-done.1 = bf16[128,1024]{1,0:T(8,128)(2,1)S(1)} collective-permute-done((bf16[128,1024]{1,0:T(8,128)(2,1)S(1)}, bf16[128,1024]{1,0:T(8,128)(2,1)S(1)}, u32[]{:S(2)}, u32[]{:S(2)}) %collective-permute-start.1) | collective-permute-done | bytes 262176 | tf_op jit(solution)/shard_map/ppermute | solution.py:16
  119.3 0.8 constant_dynamic-update-slice_fusion.5
  123.8 72.3 %all-gather.5.cloned.1.call-done = bf16[1024,1024]{0,1:T(8,128)(2,1)} async-done(((bf16[1024,8]{0,1:T(8,128)(2,1)}), bf16[1024,1024]{0,1:T(8,128)(2,1)}) %all-gather.5.cloned.1.call-update) | async-done | bytes 2097168 | tf_op jit(solution)/shard_map/all_gather | solution.py:96
  196.1 10.1 %fusion.25 = f32[512,1024]{1,0:T(8,128)} fusion(bf16[1024,1024]{0,1:T(8,128)(2,1)} %all-gather.5.cloned.1.call-done, bf16[1024,1024]{1,0:T(8,128)(2,1)} %all-gather.3.cloned.1.call-done, bf16[1024,1024]{1,0:T(8,128)(2,1)} %constant_dynamic-update-slice_fusion, s32[]{:T(128)S(6)} %select_n.43), kind=kOutput, calls=%fused_computation.41 | convolution fusion | flops 2181562368 | bytes 7340036 | tf_op jit(solution)/shard_map/dot_general | solution.py:94
  207.8 1.2 copy.29
  209.0 28.9 %reduce-scatter.5.cloned.1.call-done = f32[128,1024]{1,0:T(8,128)} async-done(((f32[512,1024]{1,0:T(8,128)}), f32[128,1024]{1,0:T(8,128)}) %reduce-scatter.5.cloned.1.call-update) | async-done | bytes 524304 | tf_op jit(solution)/shard_map/reduce_scatter | solution.py:99
  237.9 1.3 fusion.69
  239.2 1.3 multiply_reduce_fusion
  240.5 0.9 add_convert_fusion
  (67 shorter events, 13.9 us)
Async XLA Ops:
  8.0 1.4 copy-start
  8.0 52.4 %reduce-scatter.3.cloned.1.call-start = ((), (), s32[]{:S(2)}) async-start(), calls=%async_computation.3 | async-start | bytes 2621440 | tf_op jit(solution)/shard_map/reduce_scatter | solution.py:79
  11.6 0.7 copy-start.7
  16.1 0.7 copy-start.10
  16.8 4.3 %copy-start.8 = (s32[1,1,128]{2,1,0:T(1,128)S(1)}, s32[1,1,128]{2,1,0:T(1,128)}, u32[]{:S(2)}) copy-start(s32[1,1,128]{2,1,0:T(1,128)} %param.25) | copy-start | bytes 1540
  16.8 43.6 %copy-start.2 = (bf16[512,1024]{1,0:T(8,128)(2,1)S(1)}, bf16[512,1024]{1,0:T(8,128)(2,1)}, u32[]{:S(2)}) copy-start(bf16[512,1024]{1,0:T(8,128)(2,1)} %param.14) | copy-start | bytes 3145732
  19.8 43.1 %copy-start.3 = (f32[1024]{0:T(1024)S(1)}, f32[1024]{0:T(1024)}, u32[]{:S(2)}) copy-start(f32[1024]{0:T(1024)} %param.19) | copy-start | bytes 12292
  19.8 43.1 %copy-start.4 = (f32[1024]{0:T(1024)S(1)}, f32[1024]{0:T(1024)}, u32[]{:S(2)}) copy-start(f32[1024]{0:T(1024)} %param.18) | copy-start | bytes 12292
  19.8 104.0 %all-gather.3.cloned.1.call-start = ((), (), s32[]{:S(2)}) async-start(), calls=%async_computation.4 | async-start | bytes 2113536 | tf_op jit(solution)/shard_map/all_gather | solution.py:90
  20.4 175.7 %all-gather.5.cloned.1.call-start = ((), (), s32[]{:S(2)}) async-start(), calls=%async_computation.5 | async-start | bytes 2113536 | tf_op jit(solution)/shard_map/all_gather | solution.py:96
  21.0 216.9 %reduce-scatter.5.cloned.1.call-start = ((), (), s32[]{:S(2)}) async-start(), calls=%async_computation.6 | async-start | bytes 2621440 | tf_op jit(solution)/shard_map/reduce_scatter | solution.py:99
  97.4 10.8 %collective-permute-start = (bf16[128,1024]{1,0:T(8,128)(2,1)}, bf16[128,1024]{1,0:T(8,128)(2,1)S(1)}, u32[]{:S(2)}, u32[]{:S(2)}) collective-permute-start(bf16[128,1024]{1,0:T(8,128)(2,1)} %bitcast.62), channel_id=1, source_target_pairs={{0,1},{1,2},{2,3},{3,0},{4,5},{5,6},{6,7},{7,4},{8,9},{9,10},{10,1... | collective-permute-start | bytes 786440 | tf_op jit(solution)/shard_map/ppermute | solution.py:16
  108.2 9.7 %collective-permute-start.1 = (bf16[128,1024]{1,0:T(8,128)(2,1)S(1)}, bf16[128,1024]{1,0:T(8,128)(2,1)S(1)}, u32[]{:S(2)}, u32[]{:S(2)}) collective-permute-start(bf16[128,1024]{1,0:T(8,128)(2,1)S(1)} %collective-permute-done), channel_id=1, source_target_pairs={{0,1},{1,2},{2,3},{3,0},{4,5},{5,6},{6,7},{7,4},{8,9},{9,10},{10,1... | collective-permute-start | bytes 786440 | tf_op jit(solution)/shard_map/ppermute | solution.py:16
  110.1 10.0 %collective-permute-start.2 = (bf16[128,1024]{1,0:T(8,128)(2,1)}, bf16[128,1024]{1,0:T(8,128)(2,1)S(1)}, u32[]{:S(2)}, u32[]{:S(2)}) collective-permute-start(bf16[128,1024]{1,0:T(8,128)(2,1)} %bitcast.62), channel_id=1, source_target_pairs={{0,3},{1,0},{2,1},{3,2},{4,7},{5,4},{6,5},{7,6},{8,11},{9,8},{10,9... | collective-permute-start | bytes 786440 | tf_op jit(solution)/shard_map/ppermute | solution.py:18
  206.3 0.7 copy-start.9
  207.0 33.4 %copy-start.5 = (f32[1024]{0:T(1024)S(1)}, f32[1024]{0:T(1024)}, u32[]{:S(2)}) copy-start(f32[1024]{0:T(1024)} %param.23) | copy-start | bytes 12292
  207.0 33.4 %copy-start.6 = (f32[1024]{0:T(1024)S(1)}, f32[1024]{0:T(1024)}, u32[]{:S(2)}) copy-start(f32[1024]{0:T(1024)} %param.22) | copy-start | bytes 12292
  237.9 2.6 %copy-start.1 = (f32[128,1024]{1,0:T(8,128)S(1)}, f32[128,1024]{1,0:T(8,128)}, u32[]{:S(2)}) copy-start(f32[128,1024]{1,0:T(8,128)} %reduce-scatter.5.cloned.1.call-done) | copy-start | bytes 1572868
Sparse Core Ops, SparseCore 0:
  19.9 40.4 reduce-scatter.2
  206.4 31.4 reduce-scatter.4
Sparse Core Ops, SparseCore 1:
  23.4 90.7 all-gather.2
  117.2 78.9 all-gather.4
